TPU v7x, 256 devices: a whole 4x4x8 slice. The times are simulated.
256 devices in a mesh: group: 4 (over y), key: 64 (over z, x, core).
Axes of the slice: x: 4, y: 4, z: 8, core: 2. Of those that a mesh axis runs over, the one named last changes fastest.
Arguments:
- src_desc: bfloat16 [65536, 256], P(('group', 'key'))
- tgt_desc: bfloat16 [131072, 256], P('key')
- src_weight: float32 [65536], P(('group', 'key')), may hold values from 0.05 to 20
- tgt_weight: float32 [131072], P('key'), may hold values from 0.05 to 20
- tgt_dual: float32 [131072], P('key'), may hold values from -1.2 to 1.2
- pair_blocks: int32 [4, 64, 2, 64], P('group', 'key'), may hold values from 0 to 63, as said below
- pair_count: int32 [4, 64], P('group', 'key'), may hold values from 8 to 64, as said below
Outputs:
- src_dual: float32 [65536], P(('group', 'key'))
- tgt_dual_new: float32 [131072], P('key')
Inputs may be any that keep to these rules, and one draw needn't show every extreme that they name: `pair_blocks`: row 0 holds source clusters 0 to 63, row 1 target clusters 0 to 7; the live slots of one device are distinct pairs; every source cluster and every target cluster is in some live pair. `pair_count`: live slots come first.
All inputs are finite; a program needn't handle non-finite values.
Results may differ from a plain program's by a relative error of at most 0.0003.
Values may be sent and summed in bfloat16 or wider, within the bound.
No kernel may reach another device: no remote copies, remote signals or barrier semaphores. Data moves between devices by JAX's collectives and lax.ppermute only.
A program may use at most 64 MiB of HBM per device.

v0:
```python
import functools

import jax
import jax.numpy as jnp
from jax import lax
from jax.experimental import pallas as pl
from jax.experimental.pallas import tpu as pltpu
from jax.sharding import PartitionSpec as P

CLUSTER = 256
UNROLL = 4

ENTROPY = 0.05
INV_ENTROPY = 20.0
NEG_FLOOR = -1e30


def _slot_ids(ids_ref, slot, src_clusters, tgt_clusters):
    src_id = jnp.minimum(jnp.maximum(ids_ref[0, slot], 0), src_clusters - 1)
    tgt_id = jnp.minimum(jnp.maximum(ids_ref[1, slot], 0), tgt_clusters - 1)
    return src_id, tgt_id


def _block_cost(src_ref, tgt_ref, sqs_ref, sqt_ref, src_id, tgt_id, width):
    src_start = pl.multiple_of(src_id * CLUSTER, CLUSTER)
    tgt_start = pl.multiple_of(tgt_id * CLUSTER, CLUSTER)
    src_rows = src_ref[pl.ds(src_start, CLUSTER), :]
    tgt_rows = tgt_ref[pl.ds(tgt_start, CLUSTER), :]
    inner = lax.dot_general(
        tgt_rows, src_rows, (((1,), (1,)), ((), ())), preferred_element_type=jnp.float32
    )
    sq_s = sqs_ref[pl.ds(src_id, 1), :]
    sq_t = sqt_ref[pl.ds(tgt_start, CLUSTER), :]
    return (sq_s + sq_t) - (2.0 / width) * inner


def _first_kernel(ids_ref, cnt_ref, src_ref, tgt_ref, sqs_ref, sqt_ref, pot_ref, top_ref, tot_ref):
    src_clusters = sqs_ref.shape[0]
    tgt_clusters = tgt_ref.shape[0] // CLUSTER
    width = src_ref.shape[1]
    top_ref[...] = jnp.full(top_ref.shape, NEG_FLOOR, jnp.float32)
    tot_ref[...] = jnp.zeros(tot_ref.shape, jnp.float32)
    count = jnp.minimum(jnp.maximum(cnt_ref[0], 0), ids_ref.shape[1])

    def scores_of(slot):
        src_id, tgt_id = _slot_ids(ids_ref, slot, src_clusters, tgt_clusters)
        cost = _block_cost(src_ref, tgt_ref, sqs_ref, sqt_ref, src_id, tgt_id, width)
        pot = pot_ref[pl.ds(pl.multiple_of(tgt_id * CLUSTER, CLUSTER), CLUSTER), :]
        return src_id, (pot - cost) * INV_ENTROPY

    def update(src_id, scores):
        peak = jnp.max(scores, axis=0, keepdims=True)
        old_top = top_ref[pl.ds(src_id, 1), :]
        old_tot = tot_ref[pl.ds(src_id, 1), :]
        new_top = jnp.maximum(old_top, peak)
        new_tot = old_tot * jnp.exp(old_top - new_top) + jnp.sum(
            jnp.exp(scores - new_top), axis=0, keepdims=True
        )
        top_ref[pl.ds(src_id, 1), :] = new_top
        tot_ref[pl.ds(src_id, 1), :] = new_tot

    def body(trip, carry):
        blocks = [scores_of(UNROLL * trip + lane) for lane in range(UNROLL)]
        for block in blocks:
            update(*block)
        return carry

    def tail(slot, carry):
        update(*scores_of(slot))
        return carry

    lax.fori_loop(0, count // UNROLL, body, 0)
    lax.fori_loop(count // UNROLL * UNROLL, count, tail, 0)
    top_ref[...] = jnp.maximum(top_ref[...] + jnp.log(tot_ref[...]), NEG_FLOOR)


def _second_kernel(ids_ref, cnt_ref, src_ref, tgt_ref, sqs_ref, sqt_ref, dual_ref, lse_ref, top_ref, tot_ref):
    src_clusters = sqs_ref.shape[0]
    tgt_clusters = tgt_ref.shape[0] // CLUSTER
    width = src_ref.shape[1]
    lanes = top_ref.shape[1]
    top_ref[...] = jnp.full(top_ref.shape, NEG_FLOOR, jnp.float32)
    tot_ref[...] = jnp.zeros(tot_ref.shape, jnp.float32)
    count = jnp.minimum(jnp.maximum(cnt_ref[0], 0), ids_ref.shape[1])

    def scores_of(slot):
        src_id, tgt_id = _slot_ids(ids_ref, slot, src_clusters, tgt_clusters)
        cost = _block_cost(src_ref, tgt_ref, sqs_ref, sqt_ref, src_id, tgt_id, width)
        pot = dual_ref[pl.ds(src_id, 1), :]
        return tgt_id, (pot - cost) * INV_ENTROPY

    def update(tgt_id, scores):
        halves = [scores[:, part * lanes:(part + 1) * lanes] for part in range(CLUSTER // lanes)]
        tgt_rows = pl.ds(pl.multiple_of(tgt_id * CLUSTER, CLUSTER), CLUSTER)
        old_top = top_ref[tgt_rows, :]
        old_tot = tot_ref[tgt_rows, :]
        new_top = old_top
        for half in halves:
            new_top = jnp.maximum(new_top, half)
        new_tot = old_tot * jnp.exp(old_top - new_top)
        for half in halves:
            new_tot = new_tot + jnp.exp(half - new_top)
        top_ref[tgt_rows, :] = new_top
        tot_ref[tgt_rows, :] = new_tot

    def body(trip, carry):
        blocks = [scores_of(UNROLL * trip + lane) for lane in range(UNROLL)]
        for block in blocks:
            update(*block)
        return carry

    def tail(slot, carry):
        update(*scores_of(slot))
        return carry

    lax.fori_loop(0, count // UNROLL, body, 0)
    lax.fori_loop(count // UNROLL * UNROLL, count, tail, 0)
    for cluster in range(tgt_clusters):
        rows = pl.ds(cluster * CLUSTER, CLUSTER)
        lane_top = top_ref[rows, :]
        peak = jnp.max(lane_top, axis=1, keepdims=True)
        total = jnp.sum(tot_ref[rows, :] * jnp.exp(lane_top - peak), axis=1, keepdims=True)
        column = jnp.maximum(peak + jnp.log(total), NEG_FLOOR)
        wide = jnp.broadcast_to(column, (CLUSTER, 128))
        lse_ref[pl.ds(cluster, 1), :] = jnp.transpose(wide)[0:1, :]


def _sweep(kernel, out_shapes, scratch, ids, cnt, group_src, tgt_desc, sq_src, sq_tgt, pot):
    vmem = pl.BlockSpec(memory_space=pltpu.VMEM)
    smem = pl.BlockSpec(memory_space=pltpu.SMEM)
    slots = ids.shape[1]
    flops = 2 * slots * CLUSTER * CLUSTER * group_src.shape[1]
    return pl.pallas_call(
        kernel,
        out_shape=out_shapes,
        in_specs=[smem, smem, vmem, vmem, vmem, vmem, vmem],
        out_specs=tuple(vmem for _ in out_shapes),
        scratch_shapes=scratch,
        compiler_params=pltpu.CompilerParams(vmem_limit_bytes=48 * 1024 * 1024),
        cost_estimate=pl.CostEstimate(
            flops=flops,
            transcendentals=slots * CLUSTER * CLUSTER,
            bytes_accessed=group_src.size * 2 + tgt_desc.size * 2,
        ),
    )(ids, cnt, group_src, tgt_desc, sq_src, sq_tgt, pot)


def merge_lse(first, second):
    top = jnp.maximum(first, second)
    return top + jnp.log1p(jnp.exp(jnp.minimum(first, second) - top))


def butterfly(lse, weight, axis, size, index):
    bit = 1
    rows = lse.shape[0]
    while bit < size:
        perm = [(i, i ^ bit) for i in range(size)]
        other = lax.ppermute(jnp.concatenate([lse, weight], axis=0), axis, perm)
        lse = merge_lse(lse, other[:rows])
        is_low = (index & bit) == 0
        low = jnp.where(is_low, weight, other[rows:])
        high = jnp.where(is_low, other[rows:], weight)
        weight = jnp.concatenate([low, high], axis=0)
        bit *= 2
    return lse, weight


def local(src_desc, tgt_desc, src_weight, tgt_weight, tgt_dual, pair_blocks, pair_count):
    width = src_desc.shape[1]
    own_clusters = src_desc.shape[0] // CLUSTER
    key_size = lax.axis_size("key")
    src_clusters = own_clusters * key_size
    tgt_clusters = tgt_desc.shape[0] // CLUSTER
    slot_total = pair_blocks.shape[3]
    ids = pair_blocks.reshape(2, slot_total)
    cnt = pair_count.reshape(1)

    group_src = lax.all_gather(src_desc, "key", axis=0, tiled=True)
    sq_src = (jnp.sum(group_src.astype(jnp.float32) ** 2, axis=1) / width).reshape(src_clusters, CLUSTER)

    sq_tgt = (jnp.sum(tgt_desc.astype(jnp.float32) ** 2, axis=1) / width).reshape(-1, 1)
    pot_col = tgt_dual.reshape(-1, 1)

    src_shape = jax.ShapeDtypeStruct((src_clusters, CLUSTER), jnp.float32)
    local_lse, _ = _sweep(
        _first_kernel, (src_shape, src_shape), [], ids, cnt, group_src, tgt_desc, sq_src, sq_tgt, pot_col
    )
    key_index = lax.axis_index("key")
    group_lse, group_weight = butterfly(
        local_lse, src_weight.reshape(own_clusters, CLUSTER), "key", key_size, key_index
    )
    group_dual = ENTROPY * jnp.log(group_weight) - ENTROPY * group_lse
    share_start = key_index * own_clusters
    src_dual = lax.dynamic_slice_in_dim(group_dual, share_start, own_clusters, 0).reshape(-1)

    tgt_shape = jax.ShapeDtypeStruct((tgt_clusters, CLUSTER), jnp.float32)
    column = pltpu.VMEM((tgt_clusters * CLUSTER, 128), jnp.float32)
    (tgt_part,) = _sweep(
        _second_kernel, (tgt_shape,), [column, column], ids, cnt, group_src, tgt_desc, sq_src, sq_tgt, group_dual
    )
    parts = lax.all_gather(tgt_part, "group", axis=0)
    merged = parts[0]
    for index in range(1, parts.shape[0]):
        merged = merge_lse(merged, parts[index])
    tgt_lse = merged.reshape(-1)
    tgt_dual_new = ENTROPY * jnp.log(tgt_weight) - ENTROPY * tgt_lse
    return (src_dual, tgt_dual_new)


def solution(mesh):
    in_specs = (
        P(("group", "key"), None),
        P("key", None),
        P(("group", "key")),
        P("key"),
        P("key"),
        P("group", "key", None, None),
        P("group", "key"),
    )
    out_specs = (P(("group", "key")), P("key"))
    return jax.shard_map(local, mesh=mesh, in_specs=in_specs, out_specs=out_specs, check_vma=False)
```

profile of v0, /device:TPU:32, one launch (start us, length us, event | category | flops | bytes accessed | tf_op | source)
XLA Modules:
  0.0 182.2 jit_solution(13877394692784342531)
XLA Ops:
  7.2 0.0 copy-start
  7.2 0.0 copy-start.1
  7.2 0.0 all-gather.3.cloned.1.call-start
  7.2 0.7 all-gather.3.cloned.1.call-update
  7.9 1.6 multiply_reduce_fusion.1
  9.5 0.4 copy.9.sqt_ref
  10.5 1.1 copy.10.pot_ref
  11.6 0.0 copy-start.3
  11.6 84.4 %all-gather.3.cloned.1.call-done.src_ref = bf16[16384,256]{1,0:T(8,128)(2,1)} async-done(((bf16[256,256]{1,0:T(8,128)(2,1)}), bf16[16384,256]{1,0:T(8,128)(2,1)}) %all-gather.3.cloned.1.call-update) | async-done | bytes 8388624 | tf_op jit(solution)/shard_map/all_gather | solution.py:178
  96.0 5.2 %multiply_reduce_fusion = f32[16384]{0:T(1024)S(1)} fusion(bf16[16384,256]{1,0:T(8,128)(2,1)} %all-gather.3.cloned.1.call-done.src_ref), kind=kLoop, calls=%fused_computation | loop fusion | flops 12566528 | bytes 8454144 | tf_op jit(solution)/shard_map/reduce_sum | solution.py:179
  101.2 0.0 copy-done
  101.2 0.0 copy-done.1
  101.3 5.3 %shard_map.86 = (f32[64,256]{1,0:T(8,128)S(1)}, f32[64,256]{1,0:T(8,128)}) custom-call(s32[2,64]{1,0:T(2,128)S(1)} %bitcast.20, s32[1]{0:T(128)} %bitcast.18.cnt_ref, bf16[16384,256]{1,0:T(8,128)(2,1)} %all-gather.3.cloned.1.call-done.src_ref, bf16[2048,256]{1,0:T(8,128)(2,1)S(1)} %copy-done, f32[64,256]{1,0:T(8,128)S(1)} %div.18.sqs_ref, ...), custom_call_target="tpu_custom_call" | custom-call | flops 2147483648 | bytes 9437184 | tf_op jit(solution)/shard_map/pallas_call | solution.py:133
  106.6 0.0 copy-done.3
  106.6 0.6 collective-permute-start
  107.2 0.9 collective-permute-done
  108.2 3.9 %collective-permute-start.1 = (f32[66,256]{1,0:T(8,128)S(1)}, f32[66,256]{1,0:T(8,128)S(1)}, u32[]{:S(2)}, u32[]{:S(2)}) collective-permute-start(f32[66,256]{1,0:T(8,128)S(1)} %pad_maximum_fusion.3), channel_id=1, source_target_pairs={{0,2},{1,3},{2,0},{3,1},{4,6},{5,7},{6,4},{7,5},{8,10},{9,11},{10,... | collective-permute-start | bytes 202760 | tf_op jit(solution)/shard_map/ppermute | solution.py:158
  112.1 2.8 %collective-permute-done.1 = f32[66,256]{1,0:T(8,128)S(1)} collective-permute-done((f32[66,256]{1,0:T(8,128)S(1)}, f32[66,256]{1,0:T(8,128)S(1)}, u32[]{:S(2)}, u32[]{:S(2)}) %collective-permute-start.1) | collective-permute-done | bytes 67616 | tf_op jit(solution)/shard_map/ppermute | solution.py:158
  114.9 5.5 %collective-permute-start.2 = (f32[68,256]{1,0:T(8,128)S(1)}, f32[68,256]{1,0:T(8,128)S(1)}, u32[]{:S(2)}, u32[]{:S(2)}) collective-permute-start(f32[68,256]{1,0:T(8,128)S(1)} %pad_maximum_fusion.4), channel_id=1, source_target_pairs={{0,4},{1,5},{2,6},{3,7},{4,0},{5,1},{6,2},{7,3},{8,12},{9,13},{10,... | collective-permute-start | bytes 208904 | tf_op jit(solution)/shard_map/ppermute | solution.py:158
  120.4 2.3 %collective-permute-done.2 = f32[68,256]{1,0:T(8,128)S(1)} collective-permute-done((f32[68,256]{1,0:T(8,128)S(1)}, f32[68,256]{1,0:T(8,128)S(1)}, u32[]{:S(2)}, u32[]{:S(2)}) %collective-permute-start.2) | collective-permute-done | bytes 69664 | tf_op jit(solution)/shard_map/ppermute | solution.py:158
  122.9 3.0 %collective-permute-start.3 = (f32[72,256]{1,0:T(8,128)S(1)}, f32[72,256]{1,0:T(8,128)S(1)}, u32[]{:S(2)}, u32[]{:S(2)}) collective-permute-start(f32[72,256]{1,0:T(8,128)S(1)} %pad_maximum_fusion.5), channel_id=1, source_target_pairs={{0,8},{1,9},{2,10},{3,11},{4,12},{5,13},{6,14},{7,15},{8,0},{9,1},... | collective-permute-start | bytes 221192 | tf_op jit(solution)/shard_map/ppermute | solution.py:158
  125.9 2.3 %collective-permute-done.3 = f32[72,256]{1,0:T(8,128)S(1)} collective-permute-done((f32[72,256]{1,0:T(8,128)S(1)}, f32[72,256]{1,0:T(8,128)S(1)}, u32[]{:S(2)}, u32[]{:S(2)}) %collective-permute-start.3) | collective-permute-done | bytes 73760 | tf_op jit(solution)/shard_map/ppermute | solution.py:158
  128.3 5.2 %collective-permute-start.4 = (f32[80,256]{1,0:T(8,128)S(1)}, f32[80,256]{1,0:T(8,128)S(1)}, u32[]{:S(2)}, u32[]{:S(2)}) collective-permute-start(f32[80,256]{1,0:T(8,128)S(1)} %pad_maximum_fusion.1), channel_id=1, source_target_pairs={{0,16},{1,17},{2,18},{3,19},{4,20},{5,21},{6,22},{7,23},{8,24},{9,... | collective-permute-start | bytes 245768 | tf_op jit(solution)/shard_map/ppermute | solution.py:158
  133.5 2.5 %collective-permute-done.4 = f32[80,256]{1,0:T(8,128)S(1)} collective-permute-done((f32[80,256]{1,0:T(8,128)S(1)}, f32[80,256]{1,0:T(8,128)S(1)}, u32[]{:S(2)}, u32[]{:S(2)}) %collective-permute-start.4) | collective-permute-done | bytes 81952 | tf_op jit(solution)/shard_map/ppermute | solution.py:158
  136.2 3.6 %collective-permute-start.5 = (f32[96,256]{1,0:T(8,128)S(1)}, f32[96,256]{1,0:T(8,128)S(1)}, u32[]{:S(2)}, u32[]{:S(2)}) collective-permute-start(f32[96,256]{1,0:T(8,128)S(1)} %pad_maximum_fusion), channel_id=1, source_target_pairs={{0,32},{1,33},{2,34},{3,35},{4,36},{5,37},{6,38},{7,39},{8,40},{9,... | collective-permute-start | bytes 294920 | tf_op jit(solution)/shard_map/ppermute | solution.py:158
  139.7 5.1 %collective-permute-done.5 = f32[96,256]{1,0:T(8,128)S(1)} collective-permute-done((f32[96,256]{1,0:T(8,128)S(1)}, f32[96,256]{1,0:T(8,128)S(1)}, u32[]{:S(2)}, u32[]{:S(2)}) %collective-permute-start.5) | collective-permute-done | bytes 98336 | tf_op jit(solution)/shard_map/ppermute | solution.py:158
  144.8 0.1 fusion.1.dual_ref
  144.8 6.1 %shard_map.87 = f32[8,256]{1,0:T(8,128)S(1)} custom-call(s32[2,64]{1,0:T(2,128)S(1)} %bitcast.21, s32[1]{0:T(128)} %bitcast.19.cnt_ref, bf16[16384,256]{1,0:T(8,128)(2,1)} %all-gather.3.cloned.1.call-done.src_ref, bf16[2048,256]{1,0:T(8,128)(2,1)S(1)} %copy-done, f32[64,256]{1,0:T(8,128)S(1)} %div.18.sqs_ref, f32[2048,1]{1,0:T(8,128)S(1)} %copy.9.sqt_ref, ...), custom_call_target="tpu_custom_call" | custom-call | flops 2147483648 | bytes 9437184 | tf_op jit(solution)/shard_map/pallas_call | solution.py:133
  151.0 23.1 %all-gather = f32[32,256]{1,0:T(8,128)S(1)} all-gather(f32[8,256]{1,0:T(8,128)S(1)} %shard_map.87), channel_id=2, replica_groups=mesh['group'=4,'key'=64] {'group'}, dimensions={0}, use_global_device_ids=true | all-gather | bytes 40960 | tf_op jit(solution)/shard_map/all_gather | solution.py:201
  174.1 0.6 constant_dynamic-slice_fusion
  174.7 0.0 copy-done.2
  174.7 0.7 multiply_subtract_fusion
  (26 shorter events, 0.4 us)
Async XLA Ops:
  7.2 94.1 %copy-start = (bf16[2048,256]{1,0:T(8,128)(2,1)S(1)}, bf16[2048,256]{1,0:T(8,128)(2,1)}, u32[]{:S(2)}) copy-start(bf16[2048,256]{1,0:T(8,128)(2,1)} %tgt_ref.3) | copy-start | bytes 3145732
  7.2 94.1 %copy-start.1 = (s32[1,1,2,64]{3,2,1,0:T(2,128)S(1)}, s32[1,1,2,64]{3,2,1,0:T(2,128)}, u32[]{:S(2)}) copy-start(s32[1,1,2,64]{3,2,1,0:T(2,128)} %param.12) | copy-start | bytes 1540
  7.2 88.8 %all-gather.3.cloned.1.call-start = ((), (), s32[]{:S(2)}) async-start(), calls=%async_computation | async-start | bytes 8519680 | tf_op jit(solution)/shard_map/all_gather | solution.py:178
  11.6 95.0 %copy-start.3 = (f32[256]{0:T(256)S(1)}, f32[256]{0:T(256)}, u32[]{:S(2)}) copy-start(f32[256]{0:T(256)} %param.9) | copy-start | bytes 3076
  106.6 68.1 %copy-start.2 = (f32[2048]{0:T(1024)S(1)}, f32[2048]{0:T(1024)}, u32[]{:S(2)}) copy-start(f32[2048]{0:T(1024)} %param.10) | copy-start | bytes 24580
  106.6 1.6 collective-permute-start
  108.2 6.6 %collective-permute-start.1 = (f32[66,256]{1,0:T(8,128)S(1)}, f32[66,256]{1,0:T(8,128)S(1)}, u32[]{:S(2)}, u32[]{:S(2)}) collective-permute-start(f32[66,256]{1,0:T(8,128)S(1)} %pad_maximum_fusion.3), channel_id=1, source_target_pairs={{0,2},{1,3},{2,0},{3,1},{4,6},{5,7},{6,4},{7,5},{8,10},{9,11},{10,... | collective-permute-start | bytes 202760 | tf_op jit(solution)/shard_map/ppermute | solution.py:158
  114.9 7.8 %collective-permute-start.2 = (f32[68,256]{1,0:T(8,128)S(1)}, f32[68,256]{1,0:T(8,128)S(1)}, u32[]{:S(2)}, u32[]{:S(2)}) collective-permute-start(f32[68,256]{1,0:T(8,128)S(1)} %pad_maximum_fusion.4), channel_id=1, source_target_pairs={{0,4},{1,5},{2,6},{3,7},{4,0},{5,1},{6,2},{7,3},{8,12},{9,13},{10,... | collective-permute-start | bytes 208904 | tf_op jit(solution)/shard_map/ppermute | solution.py:158
  122.9 5.4 %collective-permute-start.3 = (f32[72,256]{1,0:T(8,128)S(1)}, f32[72,256]{1,0:T(8,128)S(1)}, u32[]{:S(2)}, u32[]{:S(2)}) collective-permute-start(f32[72,256]{1,0:T(8,128)S(1)} %pad_maximum_fusion.5), channel_id=1, source_target_pairs={{0,8},{1,9},{2,10},{3,11},{4,12},{5,13},{6,14},{7,15},{8,0},{9,1},... | collective-permute-start | bytes 221192 | tf_op jit(solution)/shard_map/ppermute | solution.py:158
  128.3 7.8 %collective-permute-start.4 = (f32[80,256]{1,0:T(8,128)S(1)}, f32[80,256]{1,0:T(8,128)S(1)}, u32[]{:S(2)}, u32[]{:S(2)}) collective-permute-start(f32[80,256]{1,0:T(8,128)S(1)} %pad_maximum_fusion.1), channel_id=1, source_target_pairs={{0,16},{1,17},{2,18},{3,19},{4,20},{5,21},{6,22},{7,23},{8,24},{9,... | collective-permute-start | bytes 245768 | tf_op jit(solution)/shard_map/ppermute | solution.py:158
  136.2 8.6 %collective-permute-start.5 = (f32[96,256]{1,0:T(8,128)S(1)}, f32[96,256]{1,0:T(8,128)S(1)}, u32[]{:S(2)}, u32[]{:S(2)}) collective-permute-start(f32[96,256]{1,0:T(8,128)S(1)} %pad_maximum_fusion), channel_id=1, source_target_pairs={{0,32},{1,33},{2,34},{3,35},{4,36},{5,37},{6,38},{7,39},{8,40},{9,... | collective-permute-start | bytes 294920 | tf_op jit(solution)/shard_map/ppermute | solution.py:158
Sparse Core Ops, SparseCore 0:
  10.8 85.1 all-gather.2
where the time goes:
time: 183 us; the launch traced here: 182 us
  waiting for transfers between devices  101 us (55%)
  blocking collectives  23.1 us (13%)
  starting transfers between devices  21.9 us (12%)
  between operations  14.9 us (8%)
  Pallas kernels  11.4 us (6%)
  other arithmetic  7.86 us (4%)
  local copies, waits for them, and re-layouts  2.06 us (1%)
    all_gather x1, waiting for transfers between devices, local(): group_src = lax.all_gather(src_desc, 'key', axis=0, tiled=True)  84.4 us
    all_gather x1, blocking collectives, local(): parts = lax.all_gather(tgt_part, 'group', axis=0)  23.1 us
    ppermute x6, starting transfers between devices, butterfly(): other = lax.ppermute(jnp.concatenate([lse, weight], axis=0), axis, perm)  21.8 us
    ppermute x6, waiting for transfers between devices, butterfly(): other = lax.ppermute(jnp.concatenate([lse, weight], axis=0), axis, perm)  15.9 us
    pallas_call x2, Pallas kernels, _sweep(): pl.pallas_call(kernel, out_shape=out_shapes, in_specs=[smem, smem, vmem,...  11.4 us
    reduce_sum x1, other arithmetic, local(): jnp.sum(group_src.astype(jnp.float32) ** 2, axis=1) / width  5.21 us
  transfers between devices with their start and end apart: 7, of which 7 were waited for; matrix products, arithmetic and copies ran while one was open for 2% of the time, Pallas kernels for 0%

commit v1 on v0

--- a/solution.py
+++ b/solution.py
@@ -34,10 +34,19 @@
     return (sq_s + sq_t) - (2.0 / width) * inner
 
 
-def _first_kernel(ids_ref, cnt_ref, src_ref, tgt_ref, sqs_ref, sqt_ref, pot_ref, top_ref, tot_ref):
+def _first_kernel(ids_ref, cnt_ref, src_ref, tgt_ref, sqt_ref, pot_ref, top_ref, sqs_ref, tot_ref):
     src_clusters = sqs_ref.shape[0]
     tgt_clusters = tgt_ref.shape[0] // CLUSTER
     width = src_ref.shape[1]
+
+    def norms(cluster, carry):
+        rows = src_ref[pl.ds(pl.multiple_of(cluster * CLUSTER, CLUSTER), CLUSTER), :].astype(jnp.float32)
+        squares = rows * rows
+        folded = squares[:, : width // 2] + squares[:, width // 2 :]
+        sqs_ref[pl.ds(cluster, 1), :] = jnp.sum(jnp.transpose(folded), axis=0, keepdims=True) / width
+        return carry
+
+    lax.fori_loop(0, src_clusters, norms, 0)
     top_ref[...] = jnp.full(top_ref.shape, NEG_FLOOR, jnp.float32)
     tot_ref[...] = jnp.zeros(tot_ref.shape, jnp.float32)
     count = jnp.minimum(jnp.maximum(cnt_ref[0], 0), ids_ref.shape[1])
@@ -125,15 +134,16 @@
         lse_ref[pl.ds(cluster, 1), :] = jnp.transpose(wide)[0:1, :]
 
 
-def _sweep(kernel, out_shapes, scratch, ids, cnt, group_src, tgt_desc, sq_src, sq_tgt, pot):
+def _sweep(kernel, out_shapes, scratch, *operands):
     vmem = pl.BlockSpec(memory_space=pltpu.VMEM)
     smem = pl.BlockSpec(memory_space=pltpu.SMEM)
+    ids, _, group_src, tgt_desc = operands[:4]
     slots = ids.shape[1]
     flops = 2 * slots * CLUSTER * CLUSTER * group_src.shape[1]
     return pl.pallas_call(
         kernel,
         out_shape=out_shapes,
-        in_specs=[smem, smem, vmem, vmem, vmem, vmem, vmem],
+        in_specs=[smem, smem] + [vmem] * (len(operands) - 2),
         out_specs=tuple(vmem for _ in out_shapes),
         scratch_shapes=scratch,
         compiler_params=pltpu.CompilerParams(vmem_limit_bytes=48 * 1024 * 1024),
@@ -142,7 +152,7 @@
             transcendentals=slots * CLUSTER * CLUSTER,
             bytes_accessed=group_src.size * 2 + tgt_desc.size * 2,
         ),
-    )(ids, cnt, group_src, tgt_desc, sq_src, sq_tgt, pot)
+    )(*operands)
 
 
 def merge_lse(first, second):
@@ -176,14 +186,14 @@
     cnt = pair_count.reshape(1)
 
     group_src = lax.all_gather(src_desc, "key", axis=0, tiled=True)
-    sq_src = (jnp.sum(group_src.astype(jnp.float32) ** 2, axis=1) / width).reshape(src_clusters, CLUSTER)
 
     sq_tgt = (jnp.sum(tgt_desc.astype(jnp.float32) ** 2, axis=1) / width).reshape(-1, 1)
     pot_col = tgt_dual.reshape(-1, 1)
 
     src_shape = jax.ShapeDtypeStruct((src_clusters, CLUSTER), jnp.float32)
-    local_lse, _ = _sweep(
-        _first_kernel, (src_shape, src_shape), [], ids, cnt, group_src, tgt_desc, sq_src, sq_tgt, pot_col
+    local_lse, sq_src = _sweep(
+        _first_kernel, (src_shape, src_shape), [pltpu.VMEM((src_clusters, CLUSTER), jnp.float32)],
+        ids, cnt, group_src, tgt_desc, sq_tgt, pot_col,
     )
     key_index = lax.axis_index("key")
     group_lse, group_weight = butterfly(

time: 183 us -> 183 us (level)
  the two profiles are of different devices: /device:TPU:32 before, /device:TPU:68 now
where the time goes in v1:
time: 183 us; the launch traced here: 181 us
  waiting for transfers between devices  113 us (62%)
  Pallas kernels  36 us (20%)
  between operations  15 us (8%)
  blocking collectives  11.9 us (7%)
  other arithmetic  2.64 us (1%)
  starting transfers between devices  1.92 us (1%)
    all_gather x1, waiting for transfers between devices, local(): group_src = lax.all_gather(src_desc, 'key', axis=0, tiled=True)  82.2 us
    pallas_call x2, Pallas kernels, _sweep(): pl.pallas_call(kernel, out_shape=out_shapes, in_specs=[smem, smem] + [vme...  36 us
    ppermute x6, waiting for transfers between devices, butterfly(): other = lax.ppermute(jnp.concatenate([lse, weight], axis=0), axis, perm)  29.7 us
    all_gather x1, blocking collectives, local(): parts = lax.all_gather(tgt_part, 'group', axis=0)  11.9 us
  transfers between devices with their start and end apart: 7, of which 7 were waited for; matrix products, arithmetic and copies ran while one was open for 1% of the time, Pallas kernels for 0%

profile of v1, /device:TPU:68, one launch (start us, length us, event | category | flops | bytes accessed | tf_op | source)
XLA Modules:
  0.0 181.4 jit_solution(16884164017639061231)
XLA Ops:
  7.2 0.0 copy-start
  7.2 0.0 copy-start.2
  7.2 0.0 copy-start.1
  7.2 0.0 all-gather.3.cloned.1.call-start
  7.2 0.7 all-gather.3.cloned.1.call-update
  7.9 1.6 multiply_reduce_fusion
  9.5 0.4 copy.9.sqt_ref
  10.5 0.0 copy-done.2
  10.6 0.4 copy.10.pot_ref
  10.9 82.2 %all-gather.3.cloned.1.call-done.src_ref = bf16[16384,256]{1,0:T(8,128)(2,1)} async-done(((bf16[256,256]{1,0:T(8,128)(2,1)}), bf16[16384,256]{1,0:T(8,128)(2,1)}) %all-gather.3.cloned.1.call-update) | async-done | bytes 8388624 | tf_op jit(solution)/shard_map/all_gather | solution.py:188
  93.1 0.0 copy-done
  93.1 0.0 copy-done.1
  93.1 20.5 %shard_map.86 = (f32[64,256]{1,0:T(8,128)S(1)}, f32[64,256]{1,0:T(8,128)S(1)}) custom-call(s32[2,64]{1,0:T(2,128)S(1)} %bitcast.20, s32[1]{0:T(128)} %bitcast.18.cnt_ref, bf16[16384,256]{1,0:T(8,128)(2,1)} %all-gather.3.cloned.1.call-done.src_ref, bf16[2048,256]{1,0:T(8,128)(2,1)S(1)} %copy-done, f32[2048,1]{1,0:T(8,128)S(1)} %copy.9.sqt_ref, ...), custom_call_target="tpu_custom_call" | custom-call | flops 2147483648 | bytes 9437184 | tf_op jit(solution)/shard_map/pallas_call | solution.py:143
  113.7 0.1 collective-permute-start
  113.8 1.2 collective-permute-done
  115.1 0.1 collective-permute-start.1
  115.2 4.3 %collective-permute-done.1 = f32[66,256]{1,0:T(8,128)S(1)} collective-permute-done((f32[66,256]{1,0:T(8,128)S(1)}, f32[66,256]{1,0:T(8,128)S(1)}, u32[]{:S(2)}, u32[]{:S(2)}) %collective-permute-start.1) | collective-permute-done | bytes 67616 | tf_op jit(solution)/shard_map/ppermute | solution.py:168
  119.7 1.4 collective-permute-start.2
  121.1 4.5 %collective-permute-done.2 = f32[68,256]{1,0:T(8,128)S(1)} collective-permute-done((f32[68,256]{1,0:T(8,128)S(1)}, f32[68,256]{1,0:T(8,128)S(1)}, u32[]{:S(2)}, u32[]{:S(2)}) %collective-permute-start.2) | collective-permute-done | bytes 69664 | tf_op jit(solution)/shard_map/ppermute | solution.py:168
  125.7 0.1 collective-permute-start.3
  125.8 4.3 %collective-permute-done.3 = f32[72,256]{1,0:T(8,128)S(1)} collective-permute-done((f32[72,256]{1,0:T(8,128)S(1)}, f32[72,256]{1,0:T(8,128)S(1)}, u32[]{:S(2)}, u32[]{:S(2)}) %collective-permute-start.3) | collective-permute-done | bytes 73760 | tf_op jit(solution)/shard_map/ppermute | solution.py:168
  130.2 0.1 collective-permute-start.4
  130.3 6.1 %collective-permute-done.4 = f32[80,256]{1,0:T(8,128)S(1)} collective-permute-done((f32[80,256]{1,0:T(8,128)S(1)}, f32[80,256]{1,0:T(8,128)S(1)}, u32[]{:S(2)}, u32[]{:S(2)}) %collective-permute-start.4) | collective-permute-done | bytes 81952 | tf_op jit(solution)/shard_map/ppermute | solution.py:168
  136.5 0.1 collective-permute-start.5
  136.6 9.2 %collective-permute-done.5 = f32[96,256]{1,0:T(8,128)S(1)} collective-permute-done((f32[96,256]{1,0:T(8,128)S(1)}, f32[96,256]{1,0:T(8,128)S(1)}, u32[]{:S(2)}, u32[]{:S(2)}) %collective-permute-start.5) | collective-permute-done | bytes 98336 | tf_op jit(solution)/shard_map/ppermute | solution.py:168
  145.8 0.1 fusion.1.dual_ref
  145.9 0.0 copy-start.3
  145.9 15.5 %shard_map.87 = f32[8,256]{1,0:T(8,128)S(1)} custom-call(s32[2,64]{1,0:T(2,128)S(1)} %bitcast.21, s32[1]{0:T(128)} %bitcast.19.cnt_ref, bf16[16384,256]{1,0:T(8,128)(2,1)} %all-gather.3.cloned.1.call-done.src_ref, bf16[2048,256]{1,0:T(8,128)(2,1)S(1)} %copy-done, f32[64,256]{1,0:T(8,128)S(1)} %get-tuple-element.5.sqs_ref, f32[2048,1]{1,0:T(8,128)S(1)} %copy.9.sqt_ref, ...), custom_call_target="tpu_custom_call" | custom-call | flops 2147483648 | bytes 9437184 | tf_op jit(solution)/shard_map/pallas_call | solution.py:143
  161.4 11.9 %all-gather = f32[32,256]{1,0:T(8,128)S(1)} all-gather(f32[8,256]{1,0:T(8,128)S(1)} %shard_map.87), channel_id=2, replica_groups=mesh['group'=4,'key'=64] {'group'}, dimensions={0}, use_global_device_ids=true | all-gather | bytes 40960 | tf_op jit(solution)/shard_map/all_gather | solution.py:211
  173.4 0.6 constant_dynamic-slice_fusion
  173.9 0.0 copy-done.3
  173.9 0.7 multiply_subtract_fusion
  (25 shorter events, 0.4 us)
Async XLA Ops:
  7.2 86.0 %copy-start = (bf16[2048,256]{1,0:T(8,128)(2,1)S(1)}, bf16[2048,256]{1,0:T(8,128)(2,1)}, u32[]{:S(2)}) copy-start(bf16[2048,256]{1,0:T(8,128)(2,1)} %tgt_ref.3) | copy-start | bytes 3145732
  7.2 3.4 %copy-start.2 = (f32[2048]{0:T(1024)S(1)}, f32[2048]{0:T(1024)}, u32[]{:S(2)}) copy-start(f32[2048]{0:T(1024)} %param.11) | copy-start | bytes 24580
  7.2 86.0 %copy-start.1 = (s32[1,1,2,64]{3,2,1,0:T(2,128)S(1)}, s32[1,1,2,64]{3,2,1,0:T(2,128)}, u32[]{:S(2)}) copy-start(s32[1,1,2,64]{3,2,1,0:T(2,128)} %param.12) | copy-start | bytes 1540
  7.2 85.9 %all-gather.3.cloned.1.call-start = ((), (), s32[]{:S(2)}) async-start(), calls=%async_computation | async-start | bytes 8519680 | tf_op jit(solution)/shard_map/all_gather | solution.py:188
  93.1 20.5 %copy-start.4 = (f32[256]{0:T(256)S(1)}, f32[256]{0:T(256)}, u32[]{:S(2)}) copy-start(f32[256]{0:T(256)} %param.9) | copy-start | bytes 3076
  113.7 1.4 collective-permute-start
  115.1 4.4 %collective-permute-start.1 = (f32[66,256]{1,0:T(8,128)S(1)}, f32[66,256]{1,0:T(8,128)S(1)}, u32[]{:S(2)}, u32[]{:S(2)}) collective-permute-start(f32[66,256]{1,0:T(8,128)S(1)} %pad_maximum_fusion.3), channel_id=1, source_target_pairs={{0,2},{1,3},{2,0},{3,1},{4,6},{5,7},{6,4},{7,5},{8,10},{9,11},{10,... | collective-permute-start | bytes 202760 | tf_op jit(solution)/shard_map/ppermute | solution.py:168
  119.7 5.9 %collective-permute-start.2 = (f32[68,256]{1,0:T(8,128)S(1)}, f32[68,256]{1,0:T(8,128)S(1)}, u32[]{:S(2)}, u32[]{:S(2)}) collective-permute-start(f32[68,256]{1,0:T(8,128)S(1)} %pad_maximum_fusion.4), channel_id=1, source_target_pairs={{0,4},{1,5},{2,6},{3,7},{4,0},{5,1},{6,2},{7,3},{8,12},{9,13},{10,... | collective-permute-start | bytes 208904 | tf_op jit(solution)/shard_map/ppermute | solution.py:168
  125.7 4.4 %collective-permute-start.3 = (f32[72,256]{1,0:T(8,128)S(1)}, f32[72,256]{1,0:T(8,128)S(1)}, u32[]{:S(2)}, u32[]{:S(2)}) collective-permute-start(f32[72,256]{1,0:T(8,128)S(1)} %pad_maximum_fusion.5), channel_id=1, source_target_pairs={{0,8},{1,9},{2,10},{3,11},{4,12},{5,13},{6,14},{7,15},{8,0},{9,1},... | collective-permute-start | bytes 221192 | tf_op jit(solution)/shard_map/ppermute | solution.py:168
  130.2 6.2 %collective-permute-start.4 = (f32[80,256]{1,0:T(8,128)S(1)}, f32[80,256]{1,0:T(8,128)S(1)}, u32[]{:S(2)}, u32[]{:S(2)}) collective-permute-start(f32[80,256]{1,0:T(8,128)S(1)} %pad_maximum_fusion.1), channel_id=1, source_target_pairs={{0,16},{1,17},{2,18},{3,19},{4,20},{5,21},{6,22},{7,23},{8,24},{9,... | collective-permute-start | bytes 245768 | tf_op jit(solution)/shard_map/ppermute | solution.py:168
  136.5 9.3 %collective-permute-start.5 = (f32[96,256]{1,0:T(8,128)S(1)}, f32[96,256]{1,0:T(8,128)S(1)}, u32[]{:S(2)}, u32[]{:S(2)}) collective-permute-start(f32[96,256]{1,0:T(8,128)S(1)} %pad_maximum_fusion), channel_id=1, source_target_pairs={{0,32},{1,33},{2,34},{3,35},{4,36},{5,37},{6,38},{7,39},{8,40},{9,... | collective-permute-start | bytes 294920 | tf_op jit(solution)/shard_map/ppermute | solution.py:168
  145.9 28.1 %copy-start.3 = (f32[2048]{0:T(1024)S(1)}, f32[2048]{0:T(1024)}, u32[]{:S(2)}) copy-start(f32[2048]{0:T(1024)} %param.10) | copy-start | bytes 24580
Sparse Core Ops, SparseCore 0:
  10.8 82.3 all-gather.2
